TPU v7x, 128 devices: a whole 4x4x4 slice. The times are simulated.
128 devices in a mesh: expert: 16 (over z, x), dp: 8 (over y, core).
Axes of the slice: x: 4, y: 4, z: 4, core: 2. Of those that a mesh axis runs over, the one named last changes fastest.
Arguments:
- tokens: bfloat16 [16, 480, 7168], P('expert', 'dp'), may hold values from -6 to 6
- cotangent: bfloat16 [16, 480, 7168], P('expert', 'dp'), may hold values from -1.5 to 1.5
- counts: int32 [16, 8], replicated, may hold values from 1 to 60, as said below
- w_gate: bfloat16 [16, 7168, 2048], P('expert', None, 'dp'), may hold values from -0.0625 to 0.0625
- w_up: bfloat16 [16, 7168, 2048], P('expert', None, 'dp'), may hold values from -0.0625 to 0.0625
- w_down: bfloat16 [16, 2048, 7168], P('expert', 'dp'), may hold values from -0.125 to 0.125
Outputs:
- outputs: bfloat16 [16, 480, 7168], P('expert', 'dp')
- input_grads: bfloat16 [16, 480, 7168], P('expert', 'dp')
- gate_grad: bfloat16 [16, 7168, 2048], P('expert', None, 'dp')
- up_grad: bfloat16 [16, 7168, 2048], P('expert', None, 'dp')
- down_grad: bfloat16 [16, 2048, 7168], P('expert', 'dp')
Inputs may be any that keep to these rules, and one draw needn't show every extreme that they name: For each expert e below 8, exactly one of experts e and e + 8 is hot: all its counts exceed 40 - 20 and one equals 60; every count of the other is at most 20 and one equals 20.
All inputs are finite; a program needn't handle non-finite values.
Results may differ from a plain program's by a relative error of at most 0.012.
Values may be sent and summed in bfloat16 or wider, within the bound.
No kernel may reach another device: no remote copies, remote signals or barrier semaphores. Data moves between devices by JAX's collectives and lax.ppermute only.
A program may use at most 192 MiB of HBM per device.

v0:
```python
import jax
import jax.numpy as jnp
from jax import lax
from jax.sharding import PartitionSpec as P

HOME = 40
SPILL = 20


def swapped(x, axis, distance):
    return lax.ppermute(x, axis, [(i, i ^ 1 << distance) for i in range(lax.axis_size(axis))])


def silu_slope(value):
    sigma = jax.nn.sigmoid(value)
    return sigma * (1.0 + value * (1.0 - sigma))


def contract_last(left, right):
    return lax.dot_general(
        left, right, (((1,), (1,)), ((), ())), preferred_element_type=jnp.float32
    )


def contract_first(left, right):
    return lax.dot_general(
        left, right, (((0,), (0,)), ((), ())), preferred_element_type=jnp.float32
    )


def expert_work(rows, cot_rows, gate_w, up_w, down_w):
    gate = jnp.dot(rows, gate_w, preferred_element_type=jnp.float32)
    up = jnp.dot(rows, up_w, preferred_element_type=jnp.float32)
    active = jax.nn.silu(gate)
    hidden = (active * up).astype(jnp.bfloat16)
    out_part = jnp.dot(hidden, down_w, preferred_element_type=jnp.float32)
    hidden_grad = contract_last(cot_rows, down_w)
    gate_act = (hidden_grad * up * silu_slope(gate)).astype(jnp.bfloat16)
    up_act = (hidden_grad * active).astype(jnp.bfloat16)
    in_part = contract_last(gate_act, gate_w) + contract_last(up_act, up_w)
    gate_term = contract_first(rows, gate_act)
    up_term = contract_first(rows, up_act)
    down_term = contract_first(hidden, cot_rows)
    return (out_part, in_part, gate_term, up_term, down_term)


def shards(tokens, cotangent, counts, w_gate, w_up, w_down):
    rows_in = tokens[0]
    cot_in = cotangent[0]
    gate_w = w_gate[0]
    up_w = w_up[0]
    down_w = w_down[0]
    expert_total = lax.axis_size("expert")
    expert_pos = lax.axis_index("expert")
    batch_pos = lax.axis_index("dp")
    expert_ids = jnp.arange(counts.shape[0], dtype=jnp.int32)
    batch_ids = jnp.arange(counts.shape[1], dtype=jnp.int32)
    own_counts = jnp.sum(jnp.where(expert_ids[:, None] == expert_pos, counts, 0), axis=0)
    own_total = jnp.sum(jnp.where(batch_ids == batch_pos, own_counts, 0))
    own_hot = jnp.max(own_counts) > HOME - SPILL
    slots = rows_in.shape[0]
    valid = (jnp.arange(slots, dtype=jnp.int32) < own_total)[:, None]
    masked = jnp.where(valid, rows_in, jnp.zeros_like(rows_in))
    masked_cot = jnp.where(valid, cot_in, jnp.zeros_like(cot_in))
    partner_bit = expert_total.bit_length() - 2
    border = HOME - SPILL
    got_rows, got_cot, far_gate, far_up, far_down = swapped(
        (masked[HOME:], masked_cot[HOME:], gate_w, up_w, down_w), "expert", partner_bit
    )
    region_rows = masked[border:HOME] + got_rows
    region_cot = masked_cot[border:HOME] + got_cot
    pick_gate = jnp.where(own_hot, gate_w, far_gate)
    pick_up = jnp.where(own_hot, up_w, far_up)
    pick_down = jnp.where(own_hot, down_w, far_down)
    all_home, all_region, cot_home, cot_region = (
        lax.all_gather(masked[:border], "dp", axis=0, tiled=True),
        lax.all_gather(region_rows, "dp", axis=0, tiled=True),
        lax.all_gather(masked_cot[:border], "dp", axis=0, tiled=True),
        lax.all_gather(region_cot, "dp", axis=0, tiled=True),
    )
    home_res = expert_work(all_home, cot_home, gate_w, up_w, down_w)
    region_res = expert_work(all_region, cot_region, pick_gate, pick_up, pick_down)
    home_out, region_sum_out, home_in, region_sum_in = (
        lax.psum_scatter(
            home_res[0].astype(jnp.bfloat16), "dp", scatter_dimension=0, tiled=True
        ).astype(jnp.float32),
        lax.psum_scatter(
            region_res[0].astype(jnp.bfloat16), "dp", scatter_dimension=0, tiled=True
        ).astype(jnp.float32),
        lax.psum_scatter(
            home_res[1].astype(jnp.bfloat16), "dp", scatter_dimension=0, tiled=True
        ).astype(jnp.float32),
        lax.psum_scatter(
            region_res[1].astype(jnp.bfloat16), "dp", scatter_dimension=0, tiled=True
        ).astype(jnp.float32),
    )
    region_out = region_sum_out.astype(jnp.bfloat16)
    region_in = region_sum_in.astype(jnp.bfloat16)
    blank = jnp.zeros_like(region_out)
    back_out, back_in = swapped(
        (jnp.where(own_hot, blank, region_out), jnp.where(own_hot, blank, region_in)),
        "expert",
        partner_bit,
    )
    outputs = jnp.concatenate(
        [home_out.astype(jnp.bfloat16), jnp.where(own_hot, region_out, blank), back_out], axis=0
    )
    input_grads = jnp.concatenate(
        [home_in.astype(jnp.bfloat16), jnp.where(own_hot, region_in, blank), back_in], axis=0
    )
    kept = [home_res[k] + jnp.where(own_hot, region_res[k], 0.0) for k in (2, 3, 4)]
    sending = [jnp.where(own_hot, 0.0, region_res[k]).astype(jnp.bfloat16) for k in (2, 3, 4)]
    got_gate, got_up, got_down = swapped(
        (sending[0], sending[1], sending[2]), "expert", partner_bit
    )
    gate_grad = (kept[0] + got_gate.astype(jnp.float32)).astype(jnp.bfloat16)
    up_grad = (kept[1] + got_up.astype(jnp.float32)).astype(jnp.bfloat16)
    down_grad = (kept[2] + got_down.astype(jnp.float32)).astype(jnp.bfloat16)
    return (outputs[None], input_grads[None], gate_grad[None], up_grad[None], down_grad[None])


def solution(mesh):
    placed = (
        P("expert", "dp", None),
        P("expert", "dp", None),
        P(),
        P("expert", None, "dp"),
        P("expert", None, "dp"),
        P("expert", "dp", None),
    )
    return jax.shard_map(
        shards,
        mesh=mesh,
        in_specs=placed,
        out_specs=(
            P("expert", "dp", None),
            P("expert", "dp", None),
            P("expert", None, "dp"),
            P("expert", None, "dp"),
            P("expert", "dp", None),
        ),
        check_vma=False,
    )
```

profile of v0, /device:TPU:0, one launch (start us, length us, event | category | flops | bytes accessed | tf_op | source)
XLA Modules:
  0.0 693.8 jit_solution(14175474029074275268)
XLA Ops:
  9.3 1.6 bitcast_select_fusion
  12.7 4.1 collective-permute-start.5
  16.8 8.1 %collective-permute-done.5 = bf16[20,7168]{1,0:T(8,128)(2,1)S(1)} collective-permute-done((bf16[20,7168]{1,0:T(8,128)(2,1)S(1)}, bf16[20,7168]{1,0:T(8,128)(2,1)S(1)}, u32[]{:S(2)}, u32[]{:S(2)}) %collective-permute-start.5) | collective-permute-done | bytes 286752 | tf_op jit(solution)/shard_map/ppermute | solution.py:11
  25.7 3.3 collective-permute-start
  29.1 7.5 %collective-permute-done = bf16[20,7168]{1,0:T(8,128)(2,1)S(1)} collective-permute-done((bf16[20,7168]{1,0:T(8,128)(2,1)S(1)}, bf16[20,7168]{1,0:T(8,128)(2,1)S(1)}, u32[]{:S(2)}, u32[]{:S(2)}) %collective-permute-start) | collective-permute-done | bytes 286752 | tf_op jit(solution)/shard_map/ppermute | solution.py:11
  37.4 3.0 collective-permute-start.3
  41.0 3.0 collective-permute-start.1
  46.0 4.1 reshape.24
  50.1 19.3 %all-gather.9.cloned.1.call-done = bf16[8,20,7168]{2,1,0:T(8,128)(2,1)} async-done(((bf16[1,20,7168]{2,1,0:T(8,128)(2,1)}), bf16[8,20,7168]{2,1,0:T(8,128)(2,1)}) %all-gather.9.cloned.1.call-update) | async-done | bytes 2293776 | tf_op jit(solution)/shard_map/all_gather | solution.py:76
  69.5 2.7 reshape.20
  72.2 3.0 fusion.26
  79.5 2.2 convolution_convert_fusion.1
  84.0 2.8 fusion.4
  86.8 11.6 %all-gather.15.cloned.1.call-done = bf16[8,20,7168]{2,1,0:T(8,128)(2,1)} async-done(((bf16[1,20,7168]{2,1,0:T(8,128)(2,1)}), bf16[8,20,7168]{2,1,0:T(8,128)(2,1)}) %all-gather.15.cloned.1.call-update) | async-done | bytes 2293776 | tf_op jit(solution)/shard_map/all_gather | solution.py:79
  98.4 4.1 reshape.26
  102.5 24.7 %all-gather.11.cloned.1.call-done = bf16[8,20,7168]{2,1,0:T(8,128)(2,1)} async-done(((bf16[1,20,7168]{2,1,0:T(8,128)(2,1)}), bf16[8,20,7168]{2,1,0:T(8,128)(2,1)}) %all-gather.11.cloned.1.call-update) | async-done | bytes 2293776 | tf_op jit(solution)/shard_map/all_gather | solution.py:77
  127.2 4.1 reshape.22
  131.4 4.1 fusion.12
  135.5 64.7 %collective-permute-done.2 = bf16[7168,256]{1,0:T(8,128)(2,1)} collective-permute-done((bf16[7168,256]{1,0:T(8,128)(2,1)}, bf16[7168,256]{1,0:T(8,128)(2,1)}, u32[]{:S(2)}, u32[]{:S(2)}) %collective-permute-start.2) | collective-permute-done | bytes 3670048 | tf_op jit(solution)/shard_map/ppermute | solution.py:11
  201.2 75.1 %collective-permute-done.1 = bf16[7168,256]{1,0:T(8,128)(2,1)} collective-permute-done((bf16[7168,256]{1,0:T(8,128)(2,1)}, bf16[7168,256]{1,0:T(8,128)(2,1)}, u32[]{:S(2)}, u32[]{:S(2)}) %collective-permute-start.1) | collective-permute-done | bytes 3670048 | tf_op jit(solution)/shard_map/ppermute | solution.py:11
  277.4 2.5 convolution_convert_fusion
  281.4 3.1 fusion.5
  284.5 67.3 %fusion.34 = (bf16[24,7168]{1,0:T(8,128)(2,1)S(1)}, bf16[24,7168]{1,0:T(8,128)(2,1)}, bf16[24,7168]{1,0:T(8,128)(2,1)}, bf16[24,7168]{1,0:T(8,128)(2,1)S(1)}) fusion(bf16[160,7168]{1,0:T(8,128)(2,1)} %convolution_convert_fusion, bf16[160,7168]{1,0:T(8,128)(2,1)} %convolution_convert_fusion.1, bf16[160,7168]{1,0:T(8,128)(2,1)} %fusion.5, ...), kind=kCustom, calls=%all-reduce-scatter.4 | all-reduce-scatter fusion | flops 5505025 | bytes 10551808
  353.1 1.6 slice.30
  354.7 3.6 collective-permute-start.10
  358.3 7.1 %select_convert_fusion = (bf16[256,7168]{1,0:T(8,128)(2,1)}, f32[256,7168]{1,0:T(8,128)}) fusion(pred[]{:T(512)S(6)} %gt.3, bf16[160,256]{1,0:T(8,128)(2,1)} %copy-done.12, bf16[160,7168]{1,0:T(8,128)(2,1)} %reshape.26), kind=kOutput, calls=%fused_computation.10 | convolution fusion | flops 589037568 | bytes 13385729 | tf_op jit(solution)/shard_map/dot_general | solution.py:26
  365.4 5.5 select_convert_fusion.2
  370.8 2.6 collective-permute-start.13
  373.5 5.3 select_convert_fusion.1
  378.8 2.3 collective-permute-start.16
  382.7 4.0 collective-permute-start.14
  387.4 1.9 collective-permute-start.15
  390.0 1.9 collective-permute-start.17
  391.9 7.9 %concatenate.9 = bf16[52,7168]{1,0:T(8,128)(2,1)S(1)} concatenate(bf16[4,7168]{1,0:T(4,128)(2,1)} %copy-done.19, bf16[24,7168]{1,0:T(8,128)(2,1)} %copy-done.11, bf16[24,7168]{1,0:T(8,128)(2,1)} %copy-done.10), dimensions={0} | concatenate | bytes 1490944
  400.8 1.9 collective-permute-start.11
  402.7 11.0 %collective-permute-start.9 = (bf16[256,7168]{1,0:T(8,128)(2,1)}, bf16[256,7168]{1,0:T(8,128)(2,1)}, u32[]{:S(2)}, u32[]{:S(2)}) collective-permute-start(bf16[256,7168]{1,0:T(8,128)(2,1)} %get-tuple-element.35), channel_id=1, source_target_pairs={{0,64},{8,72},{16,80},{24,88},{32,96},{40,104},{48,112},{56,120},{... | collective-permute-start | bytes 11010056 | tf_op jit(solution)/shard_map/ppermute | solution.py:11
  413.7 7.9 %concatenate.11 = bf16[52,7168]{1,0:T(8,128)(2,1)S(1)} concatenate(bf16[4,7168]{1,0:T(4,128)(2,1)} %collective-permute-done.17, bf16[24,7168]{1,0:T(8,128)(2,1)} %collective-permute-done.16, bf16[24,7168]{1,0:T(8,128)(2,1)} %get-tuple-element.13), dimensions={0} | concatenate | bytes 1490944
  422.6 3.5 collective-permute-start.8
  426.1 7.9 %concatenate.8 = bf16[52,7168]{1,0:T(8,128)(2,1)S(1)} concatenate(bf16[4,7168]{1,0:T(4,128)(2,1)} %collective-permute-done.11, bf16[24,7168]{1,0:T(8,128)(2,1)} %collective-permute-done.10, bf16[24,7168]{1,0:T(8,128)(2,1)} %get-tuple-element.12), dimensions={0} | concatenate | bytes 1490944
  434.2 3.4 collective-permute-start.6
  437.6 9.5 %concatenate.10 = bf16[52,7168]{1,0:T(8,128)(2,1)} concatenate(bf16[4,7168]{1,0:T(4,128)(2,1)} %collective-permute-done.15, bf16[24,7168]{1,0:T(8,128)(2,1)} %collective-permute-done.14, bf16[24,7168]{1,0:T(8,128)(2,1)S(1)} %get-tuple-element.14), dimensions={0} | concatenate | bytes 1490944
  448.5 210.4 %collective-permute-done.4 = bf16[20,7168]{1,0:T(8,128)(2,1)} collective-permute-done((bf16[20,7168]{1,0:T(8,128)(2,1)}, bf16[20,7168]{1,0:T(8,128)(2,1)}, u32[]{:S(2)}, u32[]{:S(2)}) %collective-permute-start.4) | collective-permute-done | bytes 286752 | tf_op jit(solution)/shard_map/ppermute | solution.py:11
  658.8 2.2 maximum_bitcast_fusion
  661.0 4.2 collective-permute-done.6
  665.2 2.3 maximum_bitcast_fusion.1
  667.6 7.9 %fusion.6 = bf16[1,256,7168]{2,1,0:T(8,128)(2,1)} fusion(bf16[256,7168]{1,0:T(8,128)(2,1)} %collective-permute-done.9, f32[256,7168]{1,0:T(8,128)} %get-tuple-element.36, bf16[160,256]{1,0:T(8,128)(2,1)S(1)} %get-tuple-element.25, bf16[160,7168]{1,0:T(8,128)(2,1)S(1)} %copy-done.9, pred[]{:T(512)S(6)} %gt.3), kind=kOutput, calls=%fused_computation.11 | convolution fusion | flops 596377600 | bytes 17055744 | tf_op jit(solution)/shard_map/dot_general | solution.py:26
  675.5 5.9 fusion.8
  681.4 5.8 fusion.7
  (99 shorter events, 24.8 us)
Async XLA Ops:
  7.2 38.8 %all-gather.13.cloned.1.call-start = ((), (), s32[]{:S(2)}) async-start(), calls=%async_computation.2 | async-start | bytes 3096576 | tf_op jit(solution)/shard_map/all_gather | solution.py:78
  11.0 33.0 %copy-start.20 = (u32[128]{0:T(128)S(1)}, u32[128]{0:T(128)}, u32[]{:S(2)}) copy-start(u32[128]{0:T(128)} %constant.32) | copy-start | bytes 1540
  11.8 57.7 %all-gather.9.cloned.1.call-start = ((), (), s32[]{:S(2)}) async-start(), calls=%async_computation | async-start | bytes 3096576 | tf_op jit(solution)/shard_map/all_gather | solution.py:76
  12.6 85.8 %all-gather.15.cloned.1.call-start = ((), (), s32[]{:S(2)}) async-start(), calls=%async_computation.3 | async-start | bytes 3096576 | tf_op jit(solution)/shard_map/all_gather | solution.py:79
  12.7 12.1 %collective-permute-start.5 = (bf16[20,7168]{1,0:T(8,128)(2,1)S(1)}, bf16[20,7168]{1,0:T(8,128)(2,1)S(1)}, u32[]{:S(2)}, u32[]{:S(2)}) collective-permute-start(bf16[20,7168]{1,0:T(8,128)(2,1)S(1)} %get-tuple-element.16), channel_id=1, source_target_pairs={{0,64},{8,72},{16,80},{24,88},{32,96},{40,104},{48,112},{56,120},{... | collective-permute-start | bytes 860168 | tf_op jit(solution)/shard_map/ppermute | solution.py:11
  25.7 101.5 %all-gather.11.cloned.1.call-start = ((), (), s32[]{:S(2)}) async-start(), calls=%async_computation.1 | async-start | bytes 3096576 | tf_op jit(solution)/shard_map/all_gather | solution.py:77
  25.7 10.8 %collective-permute-start = (bf16[20,7168]{1,0:T(8,128)(2,1)S(1)}, bf16[20,7168]{1,0:T(8,128)(2,1)S(1)}, u32[]{:S(2)}, u32[]{:S(2)}) collective-permute-start(bf16[20,7168]{1,0:T(8,128)(2,1)S(1)} %get-tuple-element.18), channel_id=1, source_target_pairs={{0,64},{8,72},{16,80},{24,88},{32,96},{40,104},{48,112},{56,120},{... | collective-permute-start | bytes 860168 | tf_op jit(solution)/shard_map/ppermute | solution.py:11
  37.4 93.9 %collective-permute-start.3 = (bf16[256,7168]{1,0:T(8,128)(2,1)}, bf16[256,7168]{1,0:T(8,128)(2,1)}, u32[]{:S(2)}, u32[]{:S(2)}) collective-permute-start(bf16[256,7168]{1,0:T(8,128)(2,1)} %bitcast.105), channel_id=1, source_target_pairs={{0,64},{8,72},{16,80},{24,88},{32,96},{40,104},{48,112},{56,120},{... | collective-permute-start | bytes 11010056 | tf_op jit(solution)/shard_map/ppermute | solution.py:11
  40.5 159.7 %collective-permute-start.2 = (bf16[7168,256]{1,0:T(8,128)(2,1)}, bf16[7168,256]{1,0:T(8,128)(2,1)}, u32[]{:S(2)}, u32[]{:S(2)}) collective-permute-start(bf16[7168,256]{1,0:T(8,128)(2,1)} %bitcast.104), channel_id=1, source_target_pairs={{0,64},{8,72},{16,80},{24,88},{32,96},{40,104},{48,112},{56,120},{... | collective-permute-start | bytes 11010056 | tf_op jit(solution)/shard_map/ppermute | solution.py:11
  41.0 235.2 %collective-permute-start.1 = (bf16[7168,256]{1,0:T(8,128)(2,1)}, bf16[7168,256]{1,0:T(8,128)(2,1)}, u32[]{:S(2)}, u32[]{:S(2)}) collective-permute-start(bf16[7168,256]{1,0:T(8,128)(2,1)} %bitcast.103), channel_id=1, source_target_pairs={{0,64},{8,72},{16,80},{24,88},{32,96},{40,104},{48,112},{56,120},{... | collective-permute-start | bytes 11010056 | tf_op jit(solution)/shard_map/ppermute | solution.py:11
  72.2 3.1 copy-start.2
  75.4 2.0 copy-start.6
  75.4 2.8 copy-start.8
  79.5 2.2 copy-start.13
  79.5 3.5 copy-start.17
  81.7 2.3 copy-start.4
  131.3 68.8 %copy-start = (bf16[160,7168]{1,0:T(8,128)(2,1)S(1)}, bf16[160,7168]{1,0:T(8,128)(2,1)}, u32[]{:S(2)}) copy-start(bf16[160,7168]{1,0:T(8,128)(2,1)} %reshape.22) | copy-start | bytes 6881284
  131.3 68.8 %copy-start.5 = (bf16[1,7168,256]{2,1,0:T(8,128)(2,1)S(1)}, bf16[1,7168,256]{2,1,0:T(8,128)(2,1)}, u32[]{:S(2)}) copy-start(bf16[1,7168,256]{2,1,0:T(8,128)(2,1)} %param.10) | copy-start | bytes 11010052
  135.4 140.8 %copy-start.3 = (bf16[1,7168,256]{2,1,0:T(8,128)(2,1)S(1)}, bf16[1,7168,256]{2,1,0:T(8,128)(2,1)}, u32[]{:S(2)}) copy-start(bf16[1,7168,256]{2,1,0:T(8,128)(2,1)} %param.9) | copy-start | bytes 11010052
  201.2 76.2 %copy-start.7 = (bf16[1,256,7168]{2,1,0:T(8,128)(2,1)S(1)}, bf16[1,256,7168]{2,1,0:T(8,128)(2,1)}, u32[]{:S(2)}) copy-start(bf16[1,256,7168]{2,1,0:T(8,128)(2,1)} %param.11) | copy-start | bytes 11010052
  277.4 2.6 copy-start.12
  277.4 4.0 copy-start.15
  351.8 13.6 %copy-start.10 = (bf16[24,7168]{1,0:T(8,128)(2,1)}, bf16[24,7168]{1,0:T(8,128)(2,1)S(1)}, u32[]{:S(2)}) copy-start(bf16[24,7168]{1,0:T(8,128)(2,1)S(1)} %get-tuple-element.11) | copy-start | bytes 1032196
  351.8 37.5 %collective-permute-start.12 = (bf16[24,7168]{1,0:T(8,128)(2,1)S(1)}, bf16[24,7168]{1,0:T(8,128)(2,1)S(1)}, u32[]{:S(2)}, u32[]{:S(2)}) collective-permute-start(bf16[24,7168]{1,0:T(8,128)(2,1)S(1)} %get-tuple-element.11), channel_id=1, source_target_pairs={{0,1},{1,2},{2,3},{3,4},{4,5},{5,6},{6,7},{8,9},{9,10},{10,11},{11... | collective-permute-start | bytes 1032200
  354.7 10.7 %copy-start.1 = (bf16[160,7168]{1,0:T(8,128)(2,1)S(1)}, bf16[160,7168]{1,0:T(8,128)(2,1)}, u32[]{:S(2)}) copy-start(bf16[160,7168]{1,0:T(8,128)(2,1)} %reshape.22) | copy-start | bytes 6881284
  354.7 10.7 %copy-start.16 = (bf16[160,256]{1,0:T(8,128)(2,1)S(1)}, bf16[160,256]{1,0:T(8,128)(2,1)}, u32[]{:S(2)}) copy-start(bf16[160,256]{1,0:T(8,128)(2,1)} %copy-done.15) | copy-start | bytes 245764
  354.7 67.9 %collective-permute-start.10 = (bf16[24,7168]{1,0:T(8,128)(2,1)}, bf16[24,7168]{1,0:T(8,128)(2,1)}, u32[]{:S(2)}, u32[]{:S(2)}) collective-permute-start(bf16[24,7168]{1,0:T(8,128)(2,1)} %get-tuple-element.12), channel_id=1, source_target_pairs={{0,1},{1,2},{2,3},{3,4},{4,5},{5,6},{6,7},{8,9},{9,10},{10,11},{11... | collective-permute-start | bytes 1032200
  370.8 16.6 %collective-permute-start.13 = (bf16[4,7168]{1,0:T(4,128)(2,1)S(1)}, bf16[4,7168]{1,0:T(4,128)(2,1)S(1)}, u32[]{:S(2)}, u32[]{:S(2)}) collective-permute-start(bf16[4,7168]{1,0:T(4,128)(2,1)S(1)} %slice.31), channel_id=1, source_target_pairs={{0,2},{1,3},{2,4},{3,5},{4,6},{5,7},{8,10},{9,11},{10,12},{11,13},... | collective-permute-start | bytes 172040
  378.8 23.9 %collective-permute-start.16 = (bf16[24,7168]{1,0:T(8,128)(2,1)}, bf16[24,7168]{1,0:T(8,128)(2,1)}, u32[]{:S(2)}, u32[]{:S(2)}) collective-permute-start(bf16[24,7168]{1,0:T(8,128)(2,1)} %get-tuple-element.13), channel_id=1, source_target_pairs={{0,1},{1,2},{2,3},{3,4},{4,5},{5,6},{6,7},{8,9},{9,10},{10,11},{11... | collective-permute-start | bytes 1032200
  382.7 51.5 %collective-permute-start.14 = (bf16[24,7168]{1,0:T(8,128)(2,1)S(1)}, bf16[24,7168]{1,0:T(8,128)(2,1)}, u32[]{:S(2)}, u32[]{:S(2)}) collective-permute-start(bf16[24,7168]{1,0:T(8,128)(2,1)S(1)} %get-tuple-element.14), channel_id=1, source_target_pairs={{0,1},{1,2},{2,3},{3,4},{4,5},{5,6},{6,7},{8,9},{9,10},{10,11},{11... | collective-permute-start | bytes 1032200
  387.4 1.9 copy-start.19
  387.4 46.6 %collective-permute-start.15 = (bf16[4,7168]{1,0:T(4,128)(2,1)}, bf16[4,7168]{1,0:T(4,128)(2,1)}, u32[]{:S(2)}, u32[]{:S(2)}) collective-permute-start(bf16[4,7168]{1,0:T(4,128)(2,1)} %slice.32), channel_id=1, source_target_pairs={{0,2},{1,3},{2,4},{3,5},{4,6},{5,7},{8,10},{9,11},{10,12},{11,13},... | collective-permute-start | bytes 172040
  389.3 0.7 copy-start.11
  390.0 10.8 %collective-permute-start.17 = (bf16[4,7168]{1,0:T(4,128)(2,1)}, bf16[4,7168]{1,0:T(4,128)(2,1)}, u32[]{:S(2)}, u32[]{:S(2)}) collective-permute-start(bf16[4,7168]{1,0:T(4,128)(2,1)} %slice.33), channel_id=1, source_target_pairs={{0,2},{1,3},{2,4},{3,5},{4,6},{5,7},{8,10},{9,11},{10,12},{11,13},... | collective-permute-start | bytes 172040
  400.8 21.8 %collective-permute-start.11 = (bf16[4,7168]{1,0:T(4,128)(2,1)}, bf16[4,7168]{1,0:T(4,128)(2,1)}, u32[]{:S(2)}, u32[]{:S(2)}) collective-permute-start(bf16[4,7168]{1,0:T(4,128)(2,1)} %slice.30), channel_id=1, source_target_pairs={{0,2},{1,3},{2,4},{3,5},{4,6},{5,7},{8,10},{9,11},{10,12},{11,13},... | collective-permute-start | bytes 172040
  402.7 264.8 %collective-permute-start.9 = (bf16[256,7168]{1,0:T(8,128)(2,1)}, bf16[256,7168]{1,0:T(8,128)(2,1)}, u32[]{:S(2)}, u32[]{:S(2)}) collective-permute-start(bf16[256,7168]{1,0:T(8,128)(2,1)} %get-tuple-element.35), channel_id=1, source_target_pairs={{0,64},{8,72},{16,80},{24,88},{32,96},{40,104},{48,112},{56,120},{... | collective-permute-start | bytes 11010056 | tf_op jit(solution)/shard_map/ppermute | solution.py:11
  422.6 252.8 %collective-permute-start.7 = (bf16[7168,256]{1,0:T(8,128)(2,1)}, bf16[7168,256]{1,0:T(8,128)(2,1)}, u32[]{:S(2)}, u32[]{:S(2)}) collective-permute-start(bf16[7168,256]{1,0:T(8,128)(2,1)} %get-tuple-element.31), channel_id=1, source_target_pairs={{0,64},{8,72},{16,80},{24,88},{32,96},{40,104},{48,112},{56,120},{... | collective-permute-start | bytes 11010056 | tf_op jit(solution)/shard_map/ppermute | solution.py:11
  422.6 258.8 %collective-permute-start.8 = (bf16[7168,256]{1,0:T(8,128)(2,1)}, bf16[7168,256]{1,0:T(8,128)(2,1)}, u32[]{:S(2)}, u32[]{:S(2)}) collective-permute-start(bf16[7168,256]{1,0:T(8,128)(2,1)} %get-tuple-element.33), channel_id=1, source_target_pairs={{0,64},{8,72},{16,80},{24,88},{32,96},{40,104},{48,112},{56,120},{... | collective-permute-start | bytes 11010056 | tf_op jit(solution)/shard_map/ppermute | solution.py:11
  434.0 224.8 %collective-permute-start.4 = (bf16[20,7168]{1,0:T(8,128)(2,1)}, bf16[20,7168]{1,0:T(8,128)(2,1)}, u32[]{:S(2)}, u32[]{:S(2)}) collective-permute-start(bf16[20,7168]{1,0:T(8,128)(2,1)} %get-tuple-element.22), channel_id=1, source_target_pairs={{0,64},{8,72},{16,80},{24,88},{32,96},{40,104},{48,112},{56,120},{... | collective-permute-start | bytes 860168 | tf_op jit(solution)/shard_map/ppermute | solution.py:11
  434.2 231.0 %collective-permute-start.6 = (bf16[20,7168]{1,0:T(8,128)(2,1)}, bf16[20,7168]{1,0:T(8,128)(2,1)}, u32[]{:S(2)}, u32[]{:S(2)}) collective-permute-start(bf16[20,7168]{1,0:T(8,128)(2,1)} %get-tuple-element.20), channel_id=1, source_target_pairs={{0,64},{8,72},{16,80},{24,88},{32,96},{40,104},{48,112},{56,120},{... | collective-permute-start | bytes 860168 | tf_op jit(solution)/shard_map/ppermute | solution.py:11
  447.1 220.4 %copy-start.9 = (bf16[160,7168]{1,0:T(8,128)(2,1)S(1)}, bf16[160,7168]{1,0:T(8,128)(2,1)}, u32[]{:S(2)}) copy-start(bf16[160,7168]{1,0:T(8,128)(2,1)} %reshape.24) | copy-start | bytes 6881284
  665.2 10.2 %slice-start.2 = ((s8[7340032]{0:T(1024)(128)(4,1)}), s8[4194304]{0:T(1024)(128)(4,1)S(1)}, s32[]{:S(2)}) async-start(s8[7340032]{0:T(1024)(128)(4,1)} %bitcast.101), calls=%async_computation.6 | async-start | bytes 8388608
  667.5 7.9 %slice-start.3 = ((s8[7340032]{0:T(1024)(128)(4,1)}), s8[3145728]{0:T(1024)(128)(4,1)S(1)}, s32[]{:S(2)}) async-start(s8[7340032]{0:T(1024)(128)(4,1)} %bitcast.101), calls=%async_computation.7 | async-start | bytes 6291456
  667.5 7.9 %copy-start.14 = (bf16[160,256]{1,0:T(8,128)(2,1)S(1)}, bf16[160,256]{1,0:T(8,128)(2,1)}, u32[]{:S(2)}) copy-start(bf16[160,256]{1,0:T(8,128)(2,1)} %copy-done.13) | copy-start | bytes 245764
  667.6 13.9 %slice-start = ((s8[7340032]{0:T(1024)(128)(4,1)}), s8[4194304]{0:T(1024)(128)(4,1)S(1)}, s32[]{:S(2)}) async-start(s8[7340032]{0:T(1024)(128)(4,1)} %bitcast.99), calls=%async_computation.4 | async-start | bytes 8388608
  675.4 6.0 slice-start.1
  675.5 6.0 copy-start.18
Sparse Core Ops, SparseCore 0:
  11.9 28.5 all-gather.12
  42.8 26.6 all-gather.8
  71.7 26.6 all-gather.14
  100.5 26.6 all-gather.10
where the time goes:
time: 696 us; the launch traced here: 694 us
  waiting for transfers between devices  426 us (61%)
  blocking collectives  67.3 us (10%)
  matrix products  62.1 us (9%)
  local copies, waits for them, and re-layouts  59.5 us (9%)
  starting transfers between devices  51.8 us (7%)
  between operations  15.4 us (2%)
  other arithmetic  12 us (2%)
    ppermute x10, waiting for transfers between devices, swapped(): lax.ppermute(x, axis, [(i, i ^ 1 << distance) for i in range(lax.axis_siz...  370 us
    unnamed x1, blocking collectives  67.3 us
    unnamed x67, local copies, waits for them, and re-layouts  59.5 us
    dot_general x6, matrix products, contract_first(): lax.dot_general(left, right, (((0,), (0,)), ((), ())), preferred_element_...  37.5 us
    ppermute x10, starting transfers between devices, swapped(): lax.ppermute(x, axis, [(i, i ^ 1 << distance) for i in range(lax.axis_siz...  32.1 us
    all_gather x1, waiting for transfers between devices, shards(): lax.all_gather(region_rows, 'dp', axis=0, tiled=True)  24.7 us
    unnamed x8, starting transfers between devices  19.6 us
    all_gather x1, waiting for transfers between devices, shards(): lax.all_gather(masked[:border], 'dp', axis=0, tiled=True)  19.3 us
  transfers between devices with their start and end apart: 22, of which 9 were waited for; matrix products, arithmetic and copies ran while one was open for 16% of the time, Pallas kernels for 0%

commit v1 on v0

--- a/solution.py
+++ b/solution.py
@@ -73,7 +73,9 @@
     pick_up = jnp.where(own_hot, up_w, far_up)
     pick_down = jnp.where(own_hot, down_w, far_down)
     all_home, all_region, cot_home, cot_region = (
-        lax.all_gather(masked[:border], "dp", axis=0, tiled=True),
+        jnp.concatenate(
+            lax.all_to_all(jnp.stack([masked[:border]] * lax.axis_size("dp")), "dp", 0, 0), axis=0
+        ),
         lax.all_gather(region_rows, "dp", axis=0, tiled=True),
         lax.all_gather(masked_cot[:border], "dp", axis=0, tiled=True),
         lax.all_gather(region_cot, "dp", axis=0, tiled=True),

time: 696 us -> 696 us (level)
  waiting for transfers between devices: 426 us -> 419 us
    all_to_all x0 -> x1, waiting for transfers between devices: none -> 28.5 us  [shards(): lax.all_to_all(jnp.stack([masked[:border]] * lax.axis_size('dp')), 'dp',...]
    all_gather x1 -> x0, waiting for transfers between devices: 19.3 us -> none  [shards(): lax.all_gather(masked[:border], 'dp', axis=0, tiled=True)]
    all_gather x1, waiting for transfers between devices: 24.7 us -> 8.97 us  [shards(): lax.all_gather(region_rows, 'dp', axis=0, tiled=True)]
    all_gather x1, waiting for transfers between devices: 11.6 us -> 0.01 us  [shards(): lax.all_gather(region_cot, 'dp', axis=0, tiled=True)]
    ppermute x10, waiting for transfers between devices: 370 us -> 381 us  [swapped(): lax.ppermute(x, axis, [(i, i ^ 1 << distance) for i in range(lax.axis_siz...]
    unnamed x67 -> x65, local copies, waits for them, and re-layouts: 59.5 us -> 54.7 us
  transfers between devices with their start and end apart: 22 -> 22, of which waited for: 9 -> 9; matrix products, arithmetic and copies ran while one was open for 16% -> 17% of each run, Pallas kernels for 0% -> 0%
where the time goes in v1:
time: 696 us; the launch traced here: 693 us
  waiting for transfers between devices  419 us (60%)
  blocking collectives  67.1 us (10%)
  matrix products  65 us (9%)
  local copies, waits for them, and re-layouts  59.3 us (9%)
  starting transfers between devices  55.5 us (8%)
  between operations  15.3 us (2%)
  other arithmetic  12 us (2%)
    ppermute x10, waiting for transfers between devices, swapped(): lax.ppermute(x, axis, [(i, i ^ 1 << distance) for i in range(lax.axis_siz...  381 us
    unnamed x1, blocking collectives  67.1 us
    unnamed x65, local copies, waits for them, and re-layouts  54.7 us
    dot_general x6, matrix products, contract_first(): lax.dot_general(left, right, (((0,), (0,)), ((), ())), preferred_element_...  37.5 us
    ppermute x10, starting transfers between devices, swapped(): lax.ppermute(x, axis, [(i, i ^ 1 << distance) for i in range(lax.axis_siz...  31.2 us
    all_to_all x1, waiting for transfers between devices, shards(): lax.all_to_all(jnp.stack([masked[:border]] * lax.axis_size('dp')), 'dp',...  28.5 us
    unnamed x8, starting transfers between devices  19.6 us
    dot_general x6, matrix products, contract_last(): lax.dot_general(left, right, (((1,), (1,)), ((), ())), preferred_element_...  16.8 us
  transfers between devices with their start and end apart: 22, of which 9 were waited for; matrix products, arithmetic and copies ran while one was open for 17% of the time, Pallas kernels for 0%

profile of v1, /device:TPU:0, one launch (start us, length us, event | category | flops | bytes accessed | tf_op | source)
XLA Modules:
  0.0 693.0 jit_solution(18427171785911707112)
XLA Ops:
  11.8 4.1 collective-permute-start.5
  15.9 8.1 %collective-permute-done.5 = bf16[20,7168]{1,0:T(8,128)(2,1)S(1)} collective-permute-done((bf16[20,7168]{1,0:T(8,128)(2,1)S(1)}, bf16[20,7168]{1,0:T(8,128)(2,1)S(1)}, u32[]{:S(2)}, u32[]{:S(2)}) %collective-permute-start.5) | collective-permute-done | bytes 286752 | tf_op jit(solution)/shard_map/ppermute | solution.py:11
  24.9 3.3 collective-permute-start
  28.2 1.8 stack.2
  30.0 4.6 all-to-all-start
  36.6 3.0 collective-permute-start.3
  40.2 3.0 collective-permute-start.1
  44.9 28.5 %all-to-all-done = bf16[8,20,7168]{2,1,0:T(8,128)(2,1)} async-done(((bf16[8,20,7168]{2,1,0:T(8,128)(2,1)}), bf16[8,20,7168]{2,1,0:T(8,128)(2,1)}, u32[]{:S(2)}, u32[]{:S(2)}) %all-to-all-start) | async-done | bytes 2293792 | tf_op jit(solution)/shard_map/all_to_all | solution.py:77
  73.4 2.8 reshape.24
  76.2 3.0 fusion.26
  80.3 4.2 reshape.28
  84.5 4.3 multiply_convert_fusion.2
  88.8 2.2 convolution_convert_fusion.1
  93.9 2.8 fusion.4
  96.7 4.2 reshape.30
  100.9 9.0 %all-gather.7.cloned.1.call-done = bf16[8,20,7168]{2,1,0:T(8,128)(2,1)} async-done(((bf16[1,20,7168]{2,1,0:T(8,128)(2,1)}), bf16[8,20,7168]{2,1,0:T(8,128)(2,1)}) %all-gather.7.cloned.1.call-update) | async-done | bytes 2293776 | tf_op jit(solution)/shard_map/all_gather | solution.py:79
  109.8 4.1 reshape.26
  114.0 6.7 collective-permute-done.3
  120.7 3.9 fusion.12
  124.6 74.7 %collective-permute-done.2 = bf16[7168,256]{1,0:T(8,128)(2,1)} collective-permute-done((bf16[7168,256]{1,0:T(8,128)(2,1)}, bf16[7168,256]{1,0:T(8,128)(2,1)}, u32[]{:S(2)}, u32[]{:S(2)}) %collective-permute-start.2) | collective-permute-done | bytes 3670048 | tf_op jit(solution)/shard_map/ppermute | solution.py:11
  200.3 76.1 %collective-permute-done.1 = bf16[7168,256]{1,0:T(8,128)(2,1)} collective-permute-done((bf16[7168,256]{1,0:T(8,128)(2,1)}, bf16[7168,256]{1,0:T(8,128)(2,1)}, u32[]{:S(2)}, u32[]{:S(2)}) %collective-permute-start.1) | collective-permute-done | bytes 3670048 | tf_op jit(solution)/shard_map/ppermute | solution.py:11
  277.6 2.6 convolution_convert_fusion
  281.6 3.1 fusion.5
  284.7 67.1 %fusion.34 = (bf16[24,7168]{1,0:T(8,128)(2,1)S(1)}, bf16[24,7168]{1,0:T(8,128)(2,1)}, bf16[24,7168]{1,0:T(8,128)(2,1)}, bf16[24,7168]{1,0:T(8,128)(2,1)S(1)}) fusion(bf16[160,7168]{1,0:T(8,128)(2,1)} %convolution_convert_fusion, bf16[160,7168]{1,0:T(8,128)(2,1)} %convolution_convert_fusion.1, bf16[160,7168]{1,0:T(8,128)(2,1)} %fusion.5, ...), kind=kCustom, calls=%all-reduce-scatter.4 | all-reduce-scatter fusion | flops 5505025 | bytes 10551808
  354.7 3.8 collective-permute-start.10
  358.5 7.1 %select_convert_fusion = (bf16[256,7168]{1,0:T(8,128)(2,1)}, f32[256,7168]{1,0:T(8,128)}) fusion(pred[]{:T(512)S(6)} %gt.3, bf16[160,256]{1,0:T(8,128)(2,1)} %copy-done.12, bf16[160,7168]{1,0:T(8,128)(2,1)} %reshape.30), kind=kOutput, calls=%fused_computation.10 | convolution fusion | flops 589037568 | bytes 13385729 | tf_op jit(solution)/shard_map/dot_general | solution.py:26
  365.6 5.5 select_convert_fusion.2
  371.1 2.5 collective-permute-start.13
  373.6 5.3 select_convert_fusion.1
  379.0 2.4 collective-permute-start.16
  382.9 3.9 collective-permute-start.14
  387.4 1.9 collective-permute-start.15
  390.1 1.9 collective-permute-start.17
  391.9 7.9 %concatenate.9 = bf16[52,7168]{1,0:T(8,128)(2,1)S(1)} concatenate(bf16[4,7168]{1,0:T(4,128)(2,1)} %copy-done.19, bf16[24,7168]{1,0:T(8,128)(2,1)} %copy-done.11, bf16[24,7168]{1,0:T(8,128)(2,1)} %copy-done.10), dimensions={0} | concatenate | bytes 1490944
  400.8 1.9 collective-permute-start.11
  402.7 10.1 %collective-permute-start.9 = (bf16[256,7168]{1,0:T(8,128)(2,1)}, bf16[256,7168]{1,0:T(8,128)(2,1)}, u32[]{:S(2)}, u32[]{:S(2)}) collective-permute-start(bf16[256,7168]{1,0:T(8,128)(2,1)} %get-tuple-element.35), channel_id=1, source_target_pairs={{0,64},{8,72},{16,80},{24,88},{32,96},{40,104},{48,112},{56,120},{... | collective-permute-start | bytes 11010056 | tf_op jit(solution)/shard_map/ppermute | solution.py:11
  412.8 7.9 %concatenate.11 = bf16[52,7168]{1,0:T(8,128)(2,1)S(1)} concatenate(bf16[4,7168]{1,0:T(4,128)(2,1)} %collective-permute-done.17, bf16[24,7168]{1,0:T(8,128)(2,1)} %collective-permute-done.16, bf16[24,7168]{1,0:T(8,128)(2,1)} %get-tuple-element.13), dimensions={0} | concatenate | bytes 1490944
  421.7 3.5 collective-permute-start.8
  425.2 7.9 %concatenate.8 = bf16[52,7168]{1,0:T(8,128)(2,1)S(1)} concatenate(bf16[4,7168]{1,0:T(4,128)(2,1)} %collective-permute-done.11, bf16[24,7168]{1,0:T(8,128)(2,1)} %collective-permute-done.10, bf16[24,7168]{1,0:T(8,128)(2,1)} %get-tuple-element.12), dimensions={0} | concatenate | bytes 1490944
  433.3 3.4 collective-permute-start.6
  436.7 9.5 %concatenate.10 = bf16[52,7168]{1,0:T(8,128)(2,1)} concatenate(bf16[4,7168]{1,0:T(4,128)(2,1)} %collective-permute-done.15, bf16[24,7168]{1,0:T(8,128)(2,1)} %collective-permute-done.14, bf16[24,7168]{1,0:T(8,128)(2,1)S(1)} %get-tuple-element.14), dimensions={0} | concatenate | bytes 1490944
  447.6 210.4 %collective-permute-done.4 = bf16[20,7168]{1,0:T(8,128)(2,1)} collective-permute-done((bf16[20,7168]{1,0:T(8,128)(2,1)}, bf16[20,7168]{1,0:T(8,128)(2,1)}, u32[]{:S(2)}, u32[]{:S(2)}) %collective-permute-start.4) | collective-permute-done | bytes 286752 | tf_op jit(solution)/shard_map/ppermute | solution.py:11
  658.0 2.2 maximum_bitcast_fusion
  660.2 4.2 collective-permute-done.6
  664.3 2.3 maximum_bitcast_fusion.1
  666.7 7.9 %fusion.6 = bf16[1,256,7168]{2,1,0:T(8,128)(2,1)} fusion(bf16[256,7168]{1,0:T(8,128)(2,1)} %collective-permute-done.9, f32[256,7168]{1,0:T(8,128)} %get-tuple-element.36, bf16[160,256]{1,0:T(8,128)(2,1)S(1)} %get-tuple-element.25, bf16[160,7168]{1,0:T(8,128)(2,1)S(1)} %copy-done.9, pred[]{:T(512)S(6)} %gt.3), kind=kOutput, calls=%fused_computation.11 | convolution fusion | flops 596377600 | bytes 17055744 | tf_op jit(solution)/shard_map/dot_general | solution.py:26
  674.6 6.0 fusion.8
  680.6 5.8 fusion.7
  (99 shorter events, 25.5 us)
Async XLA Ops:
  7.2 73.1 %all-gather.9.cloned.1.call-start = ((), (), s32[]{:S(2)}) async-start(), calls=%async_computation.2 | async-start | bytes 3096576 | tf_op jit(solution)/shard_map/all_gather | solution.py:80
  11.8 84.9 %all-gather.11.cloned.1.call-start = ((), (), s32[]{:S(2)}) async-start(), calls=%async_computation.3 | async-start | bytes 3096576 | tf_op jit(solution)/shard_map/all_gather | solution.py:81
  11.8 12.1 %collective-permute-start.5 = (bf16[20,7168]{1,0:T(8,128)(2,1)S(1)}, bf16[20,7168]{1,0:T(8,128)(2,1)S(1)}, u32[]{:S(2)}, u32[]{:S(2)}) collective-permute-start(bf16[20,7168]{1,0:T(8,128)(2,1)S(1)} %get-tuple-element.16), channel_id=1, source_target_pairs={{0,64},{8,72},{16,80},{24,88},{32,96},{40,104},{48,112},{56,120},{... | collective-permute-start | bytes 860168 | tf_op jit(solution)/shard_map/ppermute | solution.py:11
  24.9 10.8 %collective-permute-start = (bf16[20,7168]{1,0:T(8,128)(2,1)S(1)}, bf16[20,7168]{1,0:T(8,128)(2,1)S(1)}, u32[]{:S(2)}, u32[]{:S(2)}) collective-permute-start(bf16[20,7168]{1,0:T(8,128)(2,1)S(1)} %get-tuple-element.18), channel_id=1, source_target_pairs={{0,64},{8,72},{16,80},{24,88},{32,96},{40,104},{48,112},{56,120},{... | collective-permute-start | bytes 860168 | tf_op jit(solution)/shard_map/ppermute | solution.py:11
  30.0 13.1 %copy-start.20 = (u32[128]{0:T(128)S(1)}, u32[128]{0:T(128)}, u32[]{:S(2)}) copy-start(u32[128]{0:T(128)} %constant.32) | copy-start | bytes 1540
  30.0 43.4 %all-to-all-start = ((bf16[8,20,7168]{2,1,0:T(8,128)(2,1)}), bf16[8,20,7168]{2,1,0:T(8,128)(2,1)}, u32[]{:S(2)}, u32[]{:S(2)}) async-start(bf16[8,20,7168]{2,1,0:T(8,128)(2,1)} %stack.2), calls=%async_computation | async-start | bytes 5505024 | tf_op jit(solution)/shard_map/all_to_all | solution.py:77
  34.6 75.2 %all-gather.7.cloned.1.call-start = ((), (), s32[]{:S(2)}) async-start(), calls=%async_computation.1 | async-start | bytes 3096576 | tf_op jit(solution)/shard_map/all_gather | solution.py:79
  36.6 84.1 %collective-permute-start.3 = (bf16[256,7168]{1,0:T(8,128)(2,1)}, bf16[256,7168]{1,0:T(8,128)(2,1)}, u32[]{:S(2)}, u32[]{:S(2)}) collective-permute-start(bf16[256,7168]{1,0:T(8,128)(2,1)} %bitcast.103), channel_id=1, source_target_pairs={{0,64},{8,72},{16,80},{24,88},{32,96},{40,104},{48,112},{56,120},{... | collective-permute-start | bytes 11010056 | tf_op jit(solution)/shard_map/ppermute | solution.py:11
  39.6 159.7 %collective-permute-start.2 = (bf16[7168,256]{1,0:T(8,128)(2,1)}, bf16[7168,256]{1,0:T(8,128)(2,1)}, u32[]{:S(2)}, u32[]{:S(2)}) collective-permute-start(bf16[7168,256]{1,0:T(8,128)(2,1)} %bitcast.102), channel_id=1, source_target_pairs={{0,64},{8,72},{16,80},{24,88},{32,96},{40,104},{48,112},{56,120},{... | collective-permute-start | bytes 11010056 | tf_op jit(solution)/shard_map/ppermute | solution.py:11
  40.2 236.3 %collective-permute-start.1 = (bf16[7168,256]{1,0:T(8,128)(2,1)}, bf16[7168,256]{1,0:T(8,128)(2,1)}, u32[]{:S(2)}, u32[]{:S(2)}) collective-permute-start(bf16[7168,256]{1,0:T(8,128)(2,1)} %bitcast.101), channel_id=1, source_target_pairs={{0,64},{8,72},{16,80},{24,88},{32,96},{40,104},{48,112},{56,120},{... | collective-permute-start | bytes 11010056 | tf_op jit(solution)/shard_map/ppermute | solution.py:11
  76.2 3.3 copy-start.2
  84.5 4.3 copy-start.7
  88.7 2.2 copy-start.13
  88.8 4.3 copy-start.17
  88.8 2.9 copy-start.3
  91.7 2.2 copy-start.5
  114.0 85.4 %copy-start = (bf16[160,7168]{1,0:T(8,128)(2,1)S(1)}, bf16[160,7168]{1,0:T(8,128)(2,1)}, u32[]{:S(2)}) copy-start(bf16[160,7168]{1,0:T(8,128)(2,1)} %reshape.26) | copy-start | bytes 6881284
  114.0 85.4 %copy-start.6 = (bf16[1,7168,256]{2,1,0:T(8,128)(2,1)S(1)}, bf16[1,7168,256]{2,1,0:T(8,128)(2,1)}, u32[]{:S(2)}) copy-start(bf16[1,7168,256]{2,1,0:T(8,128)(2,1)} %param.10) | copy-start | bytes 11010052
  124.6 151.9 %copy-start.4 = (bf16[1,7168,256]{2,1,0:T(8,128)(2,1)S(1)}, bf16[1,7168,256]{2,1,0:T(8,128)(2,1)}, u32[]{:S(2)}) copy-start(bf16[1,7168,256]{2,1,0:T(8,128)(2,1)} %param.9) | copy-start | bytes 11010052
  200.3 77.3 %copy-start.8 = (bf16[1,256,7168]{2,1,0:T(8,128)(2,1)S(1)}, bf16[1,256,7168]{2,1,0:T(8,128)(2,1)}, u32[]{:S(2)}) copy-start(bf16[1,256,7168]{2,1,0:T(8,128)(2,1)} %param.11) | copy-start | bytes 11010052
  277.6 2.6 copy-start.12
  277.6 4.0 copy-start.15
  351.8 13.8 %copy-start.10 = (bf16[24,7168]{1,0:T(8,128)(2,1)}, bf16[24,7168]{1,0:T(8,128)(2,1)S(1)}, u32[]{:S(2)}) copy-start(bf16[24,7168]{1,0:T(8,128)(2,1)S(1)} %get-tuple-element.11) | copy-start | bytes 1032196
  351.8 37.5 %collective-permute-start.12 = (bf16[24,7168]{1,0:T(8,128)(2,1)S(1)}, bf16[24,7168]{1,0:T(8,128)(2,1)S(1)}, u32[]{:S(2)}, u32[]{:S(2)}) collective-permute-start(bf16[24,7168]{1,0:T(8,128)(2,1)S(1)} %get-tuple-element.11), channel_id=1, source_target_pairs={{0,1},{1,2},{2,3},{3,4},{4,5},{5,6},{6,7},{8,9},{9,10},{10,11},{11... | collective-permute-start | bytes 1032200
  354.7 10.9 %copy-start.1 = (bf16[160,7168]{1,0:T(8,128)(2,1)S(1)}, bf16[160,7168]{1,0:T(8,128)(2,1)}, u32[]{:S(2)}) copy-start(bf16[160,7168]{1,0:T(8,128)(2,1)} %reshape.26) | copy-start | bytes 6881284
  354.7 10.9 %copy-start.16 = (bf16[160,256]{1,0:T(8,128)(2,1)S(1)}, bf16[160,256]{1,0:T(8,128)(2,1)}, u32[]{:S(2)}) copy-start(bf16[160,256]{1,0:T(8,128)(2,1)} %copy-done.15) | copy-start | bytes 245764
  354.7 67.0 %collective-permute-start.10 = (bf16[24,7168]{1,0:T(8,128)(2,1)}, bf16[24,7168]{1,0:T(8,128)(2,1)}, u32[]{:S(2)}, u32[]{:S(2)}) collective-permute-start(bf16[24,7168]{1,0:T(8,128)(2,1)} %get-tuple-element.12), channel_id=1, source_target_pairs={{0,1},{1,2},{2,3},{3,4},{4,5},{5,6},{6,7},{8,9},{9,10},{10,11},{11... | collective-permute-start | bytes 1032200
  371.1 16.3 %collective-permute-start.13 = (bf16[4,7168]{1,0:T(4,128)(2,1)S(1)}, bf16[4,7168]{1,0:T(4,128)(2,1)S(1)}, u32[]{:S(2)}, u32[]{:S(2)}) collective-permute-start(bf16[4,7168]{1,0:T(4,128)(2,1)S(1)} %slice.31), channel_id=1, source_target_pairs={{0,2},{1,3},{2,4},{3,5},{4,6},{5,7},{8,10},{9,11},{10,12},{11,13},... | collective-permute-start | bytes 172040
  379.0 23.8 %collective-permute-start.16 = (bf16[24,7168]{1,0:T(8,128)(2,1)}, bf16[24,7168]{1,0:T(8,128)(2,1)}, u32[]{:S(2)}, u32[]{:S(2)}) collective-permute-start(bf16[24,7168]{1,0:T(8,128)(2,1)} %get-tuple-element.13), channel_id=1, source_target_pairs={{0,1},{1,2},{2,3},{3,4},{4,5},{5,6},{6,7},{8,9},{9,10},{10,11},{11... | collective-permute-start | bytes 1032200
  382.9 50.4 %collective-permute-start.14 = (bf16[24,7168]{1,0:T(8,128)(2,1)S(1)}, bf16[24,7168]{1,0:T(8,128)(2,1)}, u32[]{:S(2)}, u32[]{:S(2)}) collective-permute-start(bf16[24,7168]{1,0:T(8,128)(2,1)S(1)} %get-tuple-element.14), channel_id=1, source_target_pairs={{0,1},{1,2},{2,3},{3,4},{4,5},{5,6},{6,7},{8,9},{9,10},{10,11},{11... | collective-permute-start | bytes 1032200
  387.4 1.9 copy-start.19
  387.4 45.7 %collective-permute-start.15 = (bf16[4,7168]{1,0:T(4,128)(2,1)}, bf16[4,7168]{1,0:T(4,128)(2,1)}, u32[]{:S(2)}, u32[]{:S(2)}) collective-permute-start(bf16[4,7168]{1,0:T(4,128)(2,1)} %slice.32), channel_id=1, source_target_pairs={{0,2},{1,3},{2,4},{3,5},{4,6},{5,7},{8,10},{9,11},{10,12},{11,13},... | collective-permute-start | bytes 172040
  389.3 0.7 copy-start.11
  390.1 10.8 %collective-permute-start.17 = (bf16[4,7168]{1,0:T(4,128)(2,1)}, bf16[4,7168]{1,0:T(4,128)(2,1)}, u32[]{:S(2)}, u32[]{:S(2)}) collective-permute-start(bf16[4,7168]{1,0:T(4,128)(2,1)} %slice.33), channel_id=1, source_target_pairs={{0,2},{1,3},{2,4},{3,5},{4,6},{5,7},{8,10},{9,11},{10,12},{11,13},... | collective-permute-start | bytes 172040
  400.8 20.9 %collective-permute-start.11 = (bf16[4,7168]{1,0:T(4,128)(2,1)}, bf16[4,7168]{1,0:T(4,128)(2,1)}, u32[]{:S(2)}, u32[]{:S(2)}) collective-permute-start(bf16[4,7168]{1,0:T(4,128)(2,1)} %slice.30), channel_id=1, source_target_pairs={{0,2},{1,3},{2,4},{3,5},{4,6},{5,7},{8,10},{9,11},{10,12},{11,13},... | collective-permute-start | bytes 172040
  402.7 263.9 %collective-permute-start.9 = (bf16[256,7168]{1,0:T(8,128)(2,1)}, bf16[256,7168]{1,0:T(8,128)(2,1)}, u32[]{:S(2)}, u32[]{:S(2)}) collective-permute-start(bf16[256,7168]{1,0:T(8,128)(2,1)} %get-tuple-element.35), channel_id=1, source_target_pairs={{0,64},{8,72},{16,80},{24,88},{32,96},{40,104},{48,112},{56,120},{... | collective-permute-start | bytes 11010056 | tf_op jit(solution)/shard_map/ppermute | solution.py:11
  421.7 252.9 %collective-permute-start.7 = (bf16[7168,256]{1,0:T(8,128)(2,1)}, bf16[7168,256]{1,0:T(8,128)(2,1)}, u32[]{:S(2)}, u32[]{:S(2)}) collective-permute-start(bf16[7168,256]{1,0:T(8,128)(2,1)} %get-tuple-element.31), channel_id=1, source_target_pairs={{0,64},{8,72},{16,80},{24,88},{32,96},{40,104},{48,112},{56,120},{... | collective-permute-start | bytes 11010056 | tf_op jit(solution)/shard_map/ppermute | solution.py:11
  421.7 258.9 %collective-permute-start.8 = (bf16[7168,256]{1,0:T(8,128)(2,1)}, bf16[7168,256]{1,0:T(8,128)(2,1)}, u32[]{:S(2)}, u32[]{:S(2)}) collective-permute-start(bf16[7168,256]{1,0:T(8,128)(2,1)} %get-tuple-element.33), channel_id=1, source_target_pairs={{0,64},{8,72},{16,80},{24,88},{32,96},{40,104},{48,112},{56,120},{... | collective-permute-start | bytes 11010056 | tf_op jit(solution)/shard_map/ppermute | solution.py:11
  433.1 224.9 %collective-permute-start.4 = (bf16[20,7168]{1,0:T(8,128)(2,1)}, bf16[20,7168]{1,0:T(8,128)(2,1)}, u32[]{:S(2)}, u32[]{:S(2)}) collective-permute-start(bf16[20,7168]{1,0:T(8,128)(2,1)} %get-tuple-element.22), channel_id=1, source_target_pairs={{0,64},{8,72},{16,80},{24,88},{32,96},{40,104},{48,112},{56,120},{... | collective-permute-start | bytes 860168 | tf_op jit(solution)/shard_map/ppermute | solution.py:11
  433.3 231.1 %collective-permute-start.6 = (bf16[20,7168]{1,0:T(8,128)(2,1)}, bf16[20,7168]{1,0:T(8,128)(2,1)}, u32[]{:S(2)}, u32[]{:S(2)}) collective-permute-start(bf16[20,7168]{1,0:T(8,128)(2,1)} %get-tuple-element.20), channel_id=1, source_target_pairs={{0,64},{8,72},{16,80},{24,88},{32,96},{40,104},{48,112},{56,120},{... | collective-permute-start | bytes 860168 | tf_op jit(solution)/shard_map/ppermute | solution.py:11
  446.2 220.4 %copy-start.9 = (bf16[160,7168]{1,0:T(8,128)(2,1)S(1)}, bf16[160,7168]{1,0:T(8,128)(2,1)}, u32[]{:S(2)}) copy-start(bf16[160,7168]{1,0:T(8,128)(2,1)} %reshape.28) | copy-start | bytes 6881284
  664.3 10.2 %slice-start.2 = ((s8[7340032]{0:T(1024)(128)(4,1)}), s8[4194304]{0:T(1024)(128)(4,1)S(1)}, s32[]{:S(2)}) async-start(s8[7340032]{0:T(1024)(128)(4,1)} %bitcast.99), calls=%async_computation.6 | async-start | bytes 8388608
  666.7 7.9 %slice-start.3 = ((s8[7340032]{0:T(1024)(128)(4,1)}), s8[3145728]{0:T(1024)(128)(4,1)S(1)}, s32[]{:S(2)}) async-start(s8[7340032]{0:T(1024)(128)(4,1)} %bitcast.99), calls=%async_computation.7 | async-start | bytes 6291456
  666.7 7.9 %copy-start.14 = (bf16[160,256]{1,0:T(8,128)(2,1)S(1)}, bf16[160,256]{1,0:T(8,128)(2,1)}, u32[]{:S(2)}) copy-start(bf16[160,256]{1,0:T(8,128)(2,1)} %copy-done.13) | copy-start | bytes 245764
  666.7 13.9 %slice-start = ((s8[7340032]{0:T(1024)(128)(4,1)}), s8[4194304]{0:T(1024)(128)(4,1)S(1)}, s32[]{:S(2)}) async-start(s8[7340032]{0:T(1024)(128)(4,1)} %bitcast.97), calls=%async_computation.4 | async-start | bytes 8388608
  674.6 6.0 slice-start.1
  674.6 6.0 copy-start.18
Sparse Core Ops, SparseCore 0:
  11.9 29.1 all-gather.8
  43.3 38.1 all-gather.10
  83.7 26.0 all-gather.6
